TPU v7x, 512 devices: a whole 4x4x16 slice. The times are simulated.
512 devices in a mesh: tiles: 32 (over z, core), chan: 16 (over y, x).
Axes of the slice: x: 4, y: 4, z: 16, core: 2. Of those that a mesh axis runs over, the one named last changes fastest.
Arguments:
- atmos_state: bfloat16 [256, 192, 256], P('tiles', 'chan'), may hold values from -6 to 6
- ocean_state: bfloat16 [256, 128, 256], P('tiles', 'chan'), may hold values from -6 to 6
- atmos_weight: bfloat16 [9, 192, 192], P(None, 'chan'), may hold values from -0.15625 to 0.15625
- ocean_weight: bfloat16 [9, 128, 128], P(None, 'chan'), may hold values from -0.1875 to 0.1875
- couple_weight: bfloat16 [128, 192], P('chan'), may hold values from -0.4375 to 0.4375
- sea_mask: int32 [256], replicated, may hold values from 0 to 1, as said below
- neighbours: int32 [256, 4], replicated, may hold values from 0 to 255, as said below
- rotations: int32 [256, 4], replicated, may hold values from 0 to 7
Outputs:
- atmos_next: bfloat16 [256, 192, 256], P('tiles', 'chan')
- ocean_next: bfloat16 [192, 128, 256], P('tiles', 'chan')
Inputs may be any that keep to these rules, and one draw needn't show every extreme that they name: `sea_mask`: exactly 192 of the 256 entries are 1; the tiles of blocks 2k and 2k + 1 of 8 tiles hold exactly 12 sea tiles together, and each such block holds between 4 and 8. neighbours[t, s] lies in the block of 8 tiles that holds t, or in the block just before or just after it, cyclically over the 32 blocks.
All inputs are finite; a program needn't handle non-finite values.
Results may differ from a plain program's by a relative error of at most 0.0034.
Values may be sent and summed in bfloat16 or wider, within the bound.
No kernel may reach another device: no remote copies, remote signals or barrier semaphores. Data moves between devices by JAX's collectives and lax.ppermute only.
A program may use at most 64 MiB of HBM per device.

v0:
```python
import jax
import jax.numpy as jnp
from jax import lax
from jax.sharding import PartitionSpec as P

SIDE = 16


def padded_2(cells, sides, width):
    for axis, dim in sides:
        count = lax.axis_size(axis)
        head = lax.slice_in_dim(cells, 0, width, axis=dim)
        tail = lax.slice_in_dim(cells, cells.shape[dim] - width, cells.shape[dim], axis=dim)
        cells = jnp.concatenate(
            [
                lax.ppermute(tail, axis, [(i, (i + 1) % count) for i in range(count)]),
                cells,
                lax.ppermute(head, axis, [((i + 1) % count, i) for i in range(count)]),
            ],
            axis=dim,
        )
    return cells


def partner(value, axis, distance):
    mask = 2**distance
    pairs = [(source, source ^ mask) for source in range(lax.axis_size(axis))]
    return lax.ppermute(value, axis, pairs)


def edge_set(tile_field):
    tile_count, chan_count = (tile_field.shape[0], tile_field.shape[1])
    tile_grid = tile_field.reshape(tile_count, chan_count, SIDE, SIDE)
    return jnp.stack(
        [
            tile_grid[:, :, 0, :],
            tile_grid[:, :, :, SIDE - 1],
            tile_grid[:, :, SIDE - 1, :],
            tile_grid[:, :, :, 0],
        ],
        axis=2,
    )


def pick_rims(edge_strips, adjacent, turn_codes):
    picked = edge_strips[adjacent]
    side_index = turn_codes % 4
    chosen = picked[:, :, :, 0, :]
    for edge_id in range(1, 4):
        chosen = jnp.where(
            (side_index == edge_id)[:, :, None, None], picked[:, :, :, edge_id, :], chosen
        )
    return jnp.where((turn_codes >= 4)[:, :, None, None], chosen[..., ::-1], chosen)


def pad_tile(tile_field, rim_cells):
    tile_count, chan_count = (tile_field.shape[0], tile_field.shape[1])
    tile_grid = tile_field.reshape(tile_count, chan_count, SIDE, SIDE)
    upper_row = jnp.pad(rim_cells[:, 0], ((0, 0), (0, 0), (1, 1)))[:, :, None, :]
    bottom = jnp.pad(rim_cells[:, 2], ((0, 0), (0, 0), (1, 1)))[:, :, None, :]
    middle = jnp.concatenate(
        [rim_cells[:, 3][:, :, :, None], tile_grid, rim_cells[:, 1][:, :, :, None]], axis=3
    )
    assembled = jnp.concatenate([upper_row, middle, bottom], axis=2).reshape(
        tile_count, chan_count, (SIDE + 2) * (SIDE + 2)
    )
    return jnp.pad(assembled, ((0, 0), (0, 0), (0, 2)))


def trim_columns(accum):
    tile_count, chan_count = (accum.shape[0], accum.shape[1])
    return accum.reshape(tile_count, chan_count, SIDE, SIDE + 2)[:, :, :, :SIDE].reshape(
        tile_count, chan_count, SIDE * SIDE
    )


def conv_step(weight, accum, piece):
    row_width = SIDE + 2
    out_span = SIDE * row_width
    for tap_index in range(9):
        offset = tap_index // 3 * row_width + tap_index % 3
        accum = accum + jnp.einsum(
            "oc,bcp->bop",
            weight[tap_index],
            piece[:, :, offset : offset + out_span],
            preferred_element_type=jnp.float32,
        )
    return accum


def ocean_layer(padded, forcing, own_state, ocean_weight, couple_weight):
    tile_count = padded.shape[0]
    out_chans = ocean_weight.shape[1]
    conv_start = jnp.zeros((tile_count, out_chans, SIDE * (SIDE + 2)), jnp.float32)
    conv_accum = conv_step(
        ocean_weight, conv_start, lax.all_gather(padded, "chan", axis=1, tiled=True)
    )
    couple_accum = jnp.einsum(
        "oc,bcp->bop",
        couple_weight,
        lax.all_gather(forcing, "chan", axis=1, tiled=True),
        preferred_element_type=jnp.float32,
    )
    mixed = trim_columns(conv_accum) + couple_accum
    return (own_state.astype(jnp.float32) + jax.nn.gelu(mixed, approximate=True)).astype(
        jnp.bfloat16
    )


def local(
    atmos_state,
    ocean_state,
    atmos_weight,
    ocean_weight,
    couple_weight,
    sea_mask,
    neighbours,
    rotations,
):
    per_dev = atmos_state.shape[0]
    atmos_local = atmos_state.shape[1]
    ocean_local = ocean_state.shape[1]
    groups = lax.axis_size("tiles")
    tile_group = lax.axis_index("tiles")
    first_tile = tile_group * per_dev
    sea_here = lax.dynamic_slice_in_dim(sea_mask, first_tile, per_dev, 0)
    sea_field = ocean_state * sea_here.astype(jnp.bfloat16)[:, None, None]
    edge_strips = jnp.concatenate([edge_set(atmos_state), edge_set(sea_field)], axis=1)
    widened = padded_2(edge_strips.reshape(per_dev, -1), (("tiles", 0),), per_dev)
    widened = widened.reshape(3 * per_dev, atmos_local + ocean_local, 4, SIDE)
    adjacent = lax.dynamic_slice_in_dim(neighbours, first_tile, per_dev, 0)
    turn_codes = lax.dynamic_slice_in_dim(rotations, first_tile, per_dev, 0)
    local_adjacent = (adjacent // per_dev - tile_group + 1) % groups * per_dev + adjacent % per_dev
    rim_cells = pick_rims(widened, local_adjacent, turn_codes)
    atmos_pad = pad_tile(atmos_state, rim_cells[:, :, :atmos_local])
    atmos_start = jnp.zeros((per_dev, atmos_weight.shape[1], SIDE * (SIDE + 2)), jnp.float32)
    atmos_accum = conv_step(
        atmos_weight, atmos_start, lax.all_gather(atmos_pad, "chan", axis=1, tiled=True)
    )
    atmos_next = (
        atmos_state.astype(jnp.float32) + jax.nn.gelu(trim_columns(atmos_accum), approximate=True)
    ).astype(jnp.bfloat16)
    per_owner = per_dev * 3 // 4
    ocean_total = per_owner * groups
    counts = jnp.sum(sea_mask.reshape(groups, per_dev), axis=1)
    starts = jnp.cumsum(counts) - counts
    sea_rank = jnp.cumsum(sea_mask) - 1
    rank_spots = jnp.where(sea_mask == 1, sea_rank, ocean_total)
    tile_of_rank = (
        jnp.zeros((ocean_total,), jnp.int32)
        .at[rank_spots]
        .set(jnp.arange(sea_mask.shape[0], dtype=jnp.int32), mode="drop")
    )
    my_first = starts[tile_group]
    my_last = my_first + counts[tile_group]
    parity = tile_group % 2
    pair_base = tile_group // 2 * 2 * per_owner
    slot_ids = jnp.arange(per_owner, dtype=jnp.int32)
    ranks_send = pair_base + 2 * slot_ids + (1 - parity)
    ranks_own = pair_base + 2 * slot_ids + parity
    send_tile = jnp.clip(tile_of_rank[ranks_send] - first_tile, 0, per_dev - 1)
    own_tile = jnp.clip(tile_of_rank[ranks_own] - first_tile, 0, per_dev - 1)
    from_here = (ranks_own >= my_first) & (ranks_own < my_last)
    block_width = (ocean_local + atmos_local) * SIDE * SIDE
    sea_block = jnp.concatenate([ocean_state, atmos_next], axis=1).reshape(per_dev, block_width)
    rim_flat = rim_cells[:, :, atmos_local:].reshape(per_dev, -1)
    packed = jnp.concatenate([sea_block, rim_flat], axis=1)
    received = partner(packed[send_tile], "tiles", 0)
    own_packed = jnp.where(from_here[:, None], packed[own_tile], received)
    own_block = own_packed[:, :block_width].reshape(
        per_owner, ocean_local + atmos_local, SIDE * SIDE
    )
    own_rims = own_packed[:, block_width:].reshape(per_owner, 4, ocean_local, SIDE)
    own_state = own_block[:, :ocean_local]
    ocean_next = ocean_layer(
        pad_tile(own_state, own_rims),
        own_block[:, ocean_local:],
        own_state,
        ocean_weight,
        couple_weight,
    )
    return (atmos_next, ocean_next)


def solution(mesh):
    placed = (
        P("tiles", "chan", None),
        P("tiles", "chan", None),
        P(None, "chan", None),
        P(None, "chan", None),
        P("chan", None),
        P(),
        P(),
        P(),
    )
    return jax.shard_map(
        local,
        mesh=mesh,
        in_specs=placed,
        out_specs=(P("tiles", "chan", None), P("tiles", "chan", None)),
        check_vma=False,
    )
```

profile of v0, /device:TPU:2, one launch (start us, length us, event | category | flops | bytes accessed | tf_op | source)
XLA Modules:
  0.0 114.3 jit_solution(959433694621876811)
XLA Ops:
  0.7 0.8 dynamic-slice_convert_fusion
  1.4 0.8 broadcast_multiply_fusion
  2.2 0.3 copy.105
  2.7 1.1 copy.100
  5.1 0.3 copy.110
  5.6 8.9 %collective-permute-start.1 = (bf16[8,1280]{1,0:T(8,128)(2,1)S(1)}, bf16[8,1280]{1,0:T(8,128)(2,1)S(1)}, u32[]{:S(2)}, u32[]{:S(2)}) collective-permute-start(bf16[8,1280]{1,0:T(8,128)(2,1)S(1)} %reshape.192), channel_id=1, source_target_pairs={{16,0},{32,16},{48,32},{64,48},{80,64},{96,80},{112,96},{128,112},... | collective-permute-start | bytes 61448 | tf_op jit(solution)/shard_map/ppermute | solution.py:18
  14.5 0.3 reduce-window.21
  15.6 1.4 %scatter_custom_fusion = s32[192]{0:T(256)S(1)} fusion(s32[256]{0:T(256)S(1)} %compare_select_fusion.1, s32[256]{0:T(256)S(1)} %iota.13, s32[]{:T(128)} %constant.105.clone.1), kind=kCustom, calls=%fused_computation.181 | custom fusion | bytes 772 | tf_op jit(solution)/shard_map/scatter | solution.py:152
  17.0 0.6 gather_fusion.1
  17.6 0.6 gather_fusion.3
  18.5 0.6 dynamic_slice.19
  19.4 0.6 dynamic_slice.18
  21.5 0.3 copy.111
  21.9 0.3 copy.112
  22.4 0.6 gather_fusion
  24.0 0.5 pad_maximum_fusion
  24.5 1.6 %copy.122 = bf16[8,12,18,18]{3,2,0,1:T(8,128)(2,1)S(1)} copy(bf16[8,12,18,18]{1,3,2,0:T(8,128)(2,1)S(1)} %pad_maximum_fusion) | data formatting | bytes 124416 | tf_op jit(solution)/shard_map/concatenate | solution.py:64
  26.1 0.3 reshape.193
  26.4 25.0 %all_gather.9 = bf16[8,192,326]{2,0,1:T(8,128)(2,1)S(1)} all-gather(bf16[8,12,326]{2,0,1:T(8,128)(2,1)S(1)} %pad.24), channel_id=1, replica_groups=mesh['tiles'=32,'chan'=16] {'chan'}, dimensions={1}, use_global_device_ids=true | all-gather | bytes 1064064 | tf_op jit(solution)/shard_map/all_gather | solution.py:138
  51.5 3.0 %fusion.131 = (bf16[8,192,288]{2,0,1:T(8,128)(2,1)S(1)}, bf16[8,192,288]{2,0,1:T(8,128)(2,1)S(1)}, bf16[8,192,288]{2,0,1:T(8,128)(2,1)S(1)}, bf16[8,192,288]{2,0...) fusion(bf16[8,192,326]{2,0,1:T(8,128)(2,1)S(1)} %all_gather.9), kind=kLoop, calls=%fused_computation.184 | loop fusion | bytes 15925248 | tf_op jit(solution)/shard_map/slice | solution.py:85
  54.7 0.3 fusion.4
  55.0 0.3 fusion.6
  55.3 0.3 fusion.8
  55.5 0.3 fusion.10
  55.8 0.3 fusion.12
  56.1 0.3 fusion.14
  56.3 0.3 fusion
  56.6 0.3 fusion.42
  57.0 0.5 reshape.194
  57.5 0.3 reshape.195
  57.9 0.6 gather_fusion.4
  58.5 2.1 %collective-permute-start.2 = (bf16[6,5632]{1,0:T(8,128)(2,1)S(1)}, bf16[6,5632]{1,0:T(8,128)(2,1)S(1)}, u32[]{:S(2)}, u32[]{:S(2)}) collective-permute-start(bf16[6,5632]{1,0:T(8,128)(2,1)S(1)} %gather_fusion.4), channel_id=1, source_target_pairs={{0,16},{16,0},{32,48},{48,32},{64,80},{80,64},{96,112},{112,96},{1... | collective-permute-start | bytes 202760 | tf_op jit(solution)/shard_map/ppermute | solution.py:28
  60.6 0.7 compare_and_fusion
  61.3 0.6 gather_fusion.2
  62.7 0.4 copy.140
  63.1 0.4 copy.139
  63.4 0.4 pad_maximum_fusion.2
  64.1 22.6 %all_gather.10 = bf16[6,128,326]{2,1,0:T(8,128)(2,1)S(1)} all-gather(bf16[6,8,326]{2,1,0:T(8,128)(2,1)S(1)} %pad.27), channel_id=1, replica_groups=mesh['tiles'=32,'chan'=16] {'chan'}, dimensions={1}, use_global_device_ids=true | all-gather | bytes 532032 | tf_op jit(solution)/shard_map/all_gather | solution.py:96
  86.9 0.4 convolution_add_fusion.7
  87.2 0.4 convolution_add_fusion.6
  87.6 0.4 convolution_add_fusion.5
  87.9 0.4 convolution_add_fusion.4
  88.3 0.4 convolution_add_fusion.3
  88.6 0.4 convolution_add_fusion.2
  89.0 0.4 convolution_add_fusion.1
  89.4 0.4 fusion.45
  90.2 23.3 %all_gather.11 = bf16[6,192,256]{2,0,1:T(8,128)(2,1)S(1)} all-gather(bf16[6,12,256]{2,0,1:T(8,128)(2,1)S(1)} %copy.153), channel_id=1, replica_groups=mesh['tiles'=32,'chan'=16] {'chan'}, dimensions={1}, use_global_device_ids=true | all-gather | bytes 626688 | tf_op jit(solution)/shard_map/all_gather | solution.py:101
  113.5 0.8 add_convert_fusion
  (100 shorter events, 6.0 us)
Async XLA Ops:
  0.6 112.9 %copy-start = (bf16[8,192]{1,0:T(8,128)(2,1)S(1)}, bf16[8,192]{1,0:T(8,128)(2,1)}, u32[]{:S(2)}) copy-start(bf16[8,192]{1,0:T(8,128)(2,1)} %param.12) | copy-start | bytes 9220
  2.7 11.9 %copy-start.5 = (s32[256]{0:T(256)S(1)}, s32[256]{0:T(256)}, u32[]{:S(2)}) copy-start(s32[256]{0:T(256)} %param.13) | copy-start | bytes 3076
  2.7 12.5 %copy-start.6 = (s32[256,4]{0,1:T(4,128)S(1)}, s32[256,4]{0,1:T(4,128)}, u32[]{:S(2)}) copy-start(s32[256,4]{0,1:T(4,128)} %param.14) | copy-start | bytes 12292
  2.7 12.7 %copy-start.7 = (s32[256,4]{0,1:T(4,128)S(1)}, s32[256,4]{0,1:T(4,128)}, u32[]{:S(2)}) copy-start(s32[256,4]{0,1:T(4,128)} %param.15) | copy-start | bytes 12292
  4.4 14.0 %copy-start.3 = (bf16[8,8,256]{2,1,0:T(8,128)(2,1)S(1)}, bf16[8,8,256]{2,1,0:T(8,128)(2,1)}, u32[]{:S(2)}) copy-start(bf16[8,8,256]{2,1,0:T(8,128)(2,1)} %param.9) | copy-start | bytes 98308
  5.6 16.2 %collective-permute-start.1 = (bf16[8,1280]{1,0:T(8,128)(2,1)S(1)}, bf16[8,1280]{1,0:T(8,128)(2,1)S(1)}, u32[]{:S(2)}, u32[]{:S(2)}) collective-permute-start(bf16[8,1280]{1,0:T(8,128)(2,1)S(1)} %reshape.192), channel_id=1, source_target_pairs={{16,0},{32,16},{48,32},{64,48},{80,64},{96,80},{112,96},{128,112},... | collective-permute-start | bytes 61448 | tf_op jit(solution)/shard_map/ppermute | solution.py:18
  14.5 6.8 %collective-permute-start = (bf16[8,1280]{1,0:T(8,128)(2,1)S(1)}, bf16[8,1280]{1,0:T(8,128)(2,1)S(1)}, u32[]{:S(2)}, u32[]{:S(2)}) collective-permute-start(bf16[8,1280]{1,0:T(8,128)(2,1)S(1)} %reshape.192), channel_id=1, source_target_pairs={{0,16},{16,32},{32,48},{48,64},{64,80},{80,96},{96,112},{112,128},... | collective-permute-start | bytes 61448 | tf_op jit(solution)/shard_map/ppermute | solution.py:16
  51.5 3.0 %copy-start.8 = (bf16[9,12,192]{2,1,0:T(8,128)(2,1)S(1)}, bf16[9,12,192]{2,1,0:T(8,128)(2,1)}, u32[]{:S(2)}) copy-start(bf16[9,12,192]{2,1,0:T(8,128)(2,1)} %param.10) | copy-start | bytes 124420
  56.9 0.9 copy-start.1
  57.9 4.1 %copy-start.2 = (bf16[8,12,256]{2,0,1:T(8,128)(2,1)}, bf16[8,12,256]{2,0,1:T(8,128)(2,1)S(1)}, u32[]{:S(2)}) copy-start(bf16[8,12,256]{2,0,1:T(8,128)(2,1)S(1)} %fusion.69) | copy-start | bytes 147460
  58.5 3.4 %collective-permute-start.2 = (bf16[6,5632]{1,0:T(8,128)(2,1)S(1)}, bf16[6,5632]{1,0:T(8,128)(2,1)S(1)}, u32[]{:S(2)}, u32[]{:S(2)}) collective-permute-start(bf16[6,5632]{1,0:T(8,128)(2,1)S(1)} %gather_fusion.4), channel_id=1, source_target_pairs={{0,16},{16,0},{32,48},{48,32},{64,80},{80,64},{96,112},{112,96},{1... | collective-permute-start | bytes 202760 | tf_op jit(solution)/shard_map/ppermute | solution.py:28
  62.7 24.0 %copy-start.4 = (bf16[9,8,128]{2,1,0:T(8,128)(2,1)S(1)}, bf16[9,8,128]{2,1,0:T(8,128)(2,1)}, u32[]{:S(2)}) copy-start(bf16[9,8,128]{2,1,0:T(8,128)(2,1)} %param.11) | copy-start | bytes 55300
where the time goes:
time: 115 us; the launch traced here: 114 us
  blocking collectives  71 us (62%)
  local copies, waits for them, and re-layouts  18.7 us (16%)
  starting transfers between devices  11.1 us (10%)
  matrix products  6.31 us (5%)
  other arithmetic  4.8 us (4%)
  between operations  2.53 us (2%)
    all_gather x1, blocking collectives, local(): lax.all_gather(atmos_pad, 'chan', axis=1, tiled=True)  25 us
    all_gather x1, blocking collectives, ocean_layer(): lax.all_gather(forcing, 'chan', axis=1, tiled=True)  23.3 us
    all_gather x1, blocking collectives, ocean_layer(): lax.all_gather(padded, 'chan', axis=1, tiled=True)  22.6 us
    ppermute x1, starting transfers between devices, padded_2(): lax.ppermute(head, axis, [((i + 1) % count, i) for i in range(count)])  8.95 us
    dot_general x18, matrix products, conv_step(): jnp.einsum('oc,bcp->bop', weight[tap_index], piece[:, :, offset:offset +...  5.48 us
    slice x1, local copies, waits for them, and re-layouts, conv_step(): piece[:, :, offset:offset + out_span]  2.97 us
  transfers between devices with their start and end apart: 3, of which 0 were waited for; matrix products, arithmetic and copies ran while one was open for 6% of the time, Pallas kernels for 0%

commit v1 on v0

--- a/solution.py
+++ b/solution.py
@@ -4,6 +4,13 @@
 from jax.sharding import PartitionSpec as P
 
 SIDE = 16
+
+
+def all_by_exchange(array, axis, along):
+    count = lax.axis_size(axis)
+    blocks = jnp.stack([array for _ in range(count)])
+    blocks = lax.all_to_all(blocks, axis, split_axis=0, concat_axis=0)
+    return jnp.concatenate(blocks, axis=along)
 
 
 def padded_2(cells, sides, width):
@@ -134,9 +141,7 @@
     rim_cells = pick_rims(widened, local_adjacent, turn_codes)
     atmos_pad = pad_tile(atmos_state, rim_cells[:, :, :atmos_local])
     atmos_start = jnp.zeros((per_dev, atmos_weight.shape[1], SIDE * (SIDE + 2)), jnp.float32)
-    atmos_accum = conv_step(
-        atmos_weight, atmos_start, lax.all_gather(atmos_pad, "chan", axis=1, tiled=True)
-    )
+    atmos_accum = conv_step(atmos_weight, atmos_start, all_by_exchange(atmos_pad, "chan", 1))
     atmos_next = (
         atmos_state.astype(jnp.float32) + jax.nn.gelu(trim_columns(atmos_accum), approximate=True)
     ).astype(jnp.bfloat16)

time: 115 us -> 110 us (0.957)
  blocking collectives: 71 us -> 45 us
  waiting for transfers between devices: 0.01 us -> 12.4 us
  starting transfers between devices: 11.1 us -> 18.7 us
    all_gather x1 -> x0, blocking collectives: 25 us -> none  [local(): lax.all_gather(atmos_pad, 'chan', axis=1, tiled=True)]
    all_to_all x0 -> x1, waiting for transfers between devices: none -> 8.87 us  [all_by_exchange(): blocks = lax.all_to_all(blocks, axis, split_axis=0, concat_axis=0)]
    all_to_all x0 -> x1, starting transfers between devices: none -> 7.61 us  [all_by_exchange(): blocks = lax.all_to_all(blocks, axis, split_axis=0, concat_axis=0)]
    ppermute x1, waiting for transfers between devices: 0.01 us -> 3.51 us  [padded_2(): lax.ppermute(tail, axis, [(i, (i + 1) % count) for i in range(count)])]
  transfers between devices with their start and end apart: 3 -> 4, of which waited for: 0 -> 2; matrix products, arithmetic and copies ran while one was open for 6% -> 7% of each run, Pallas kernels for 0% -> 0%
where the time goes in v1:
time: 110 us; the launch traced here: 109 us
  blocking collectives  45 us (41%)
  local copies, waits for them, and re-layouts  19.8 us (18%)
  starting transfers between devices  18.7 us (17%)
  waiting for transfers between devices  12.4 us (11%)
  matrix products  6.31 us (6%)
  other arithmetic  4.78 us (4%)
  between operations  2.54 us (2%)
    all_gather x1, blocking collectives, ocean_layer(): lax.all_gather(forcing, 'chan', axis=1, tiled=True)  22.6 us
    all_gather x1, blocking collectives, ocean_layer(): lax.all_gather(padded, 'chan', axis=1, tiled=True)  22.5 us
    ppermute x1, starting transfers between devices, padded_2(): lax.ppermute(head, axis, [((i + 1) % count, i) for i in range(count)])  8.95 us
    all_to_all x1, waiting for transfers between devices, all_by_exchange(): blocks = lax.all_to_all(blocks, axis, split_axis=0, concat_axis=0)  8.87 us
    all_to_all x1, starting transfers between devices, all_by_exchange(): blocks = lax.all_to_all(blocks, axis, split_axis=0, concat_axis=0)  7.61 us
    dot_general x18, matrix products, conv_step(): jnp.einsum('oc,bcp->bop', weight[tap_index], piece[:, :, offset:offset +...  5.48 us
    ppermute x1, waiting for transfers between devices, padded_2(): lax.ppermute(tail, axis, [(i, (i + 1) % count) for i in range(count)])  3.51 us
    slice x1, local copies, waits for them, and re-layouts, conv_step(): piece[:, :, offset:offset + out_span]  2.95 us
  transfers between devices with their start and end apart: 4, of which 2 were waited for; matrix products, arithmetic and copies ran while one was open for 7% of the time, Pallas kernels for 0%

profile of v1, /device:TPU:2, one launch (start us, length us, event | category | flops | bytes accessed | tf_op | source)
XLA Modules:
  0.0 109.5 jit_solution(18361998096521599721)
XLA Ops:
  0.7 0.8 dynamic-slice_convert_fusion
  1.4 0.8 broadcast_multiply_fusion
  2.2 0.3 copy.124
  2.7 1.1 %copy.119 = bf16[8,12,256]{1,2,0:T(8,128)(2,1)S(1)} copy(bf16[8,12,256]{2,0,1:T(8,128)(2,1)} %param.8) | data formatting | bytes 98304 | tf_op args[0]
  5.0 0.3 copy.129
  5.5 8.9 %collective-permute-start.1 = (bf16[8,1280]{1,0:T(8,128)(2,1)S(1)}, bf16[8,1280]{1,0:T(8,128)(2,1)S(1)}, u32[]{:S(2)}, u32[]{:S(2)}) collective-permute-start(bf16[8,1280]{1,0:T(8,128)(2,1)S(1)} %reshape.200), channel_id=1, source_target_pairs={{16,0},{32,16},{48,32},{64,48},{80,64},{96,80},{112,96},{128,112},... | collective-permute-start | bytes 61448 | tf_op jit(solution)/shard_map/ppermute | solution.py:25
  14.5 0.3 reduce-window.21
  15.4 3.5 %collective-permute-done = bf16[8,1280]{1,0:T(8,128)(2,1)S(1)} collective-permute-done((bf16[8,1280]{1,0:T(8,128)(2,1)S(1)}, bf16[8,1280]{1,0:T(8,128)(2,1)S(1)}, u32[]{:S(2)}, u32[]{:S(2)}) %collective-permute-start) | collective-permute-done | bytes 20512 | tf_op jit(solution)/shard_map/ppermute | solution.py:23
  19.1 0.3 copy.130
  19.6 0.3 copy.131
  20.0 0.6 gather_fusion
  21.3 0.5 pad_maximum_fusion
  21.8 1.6 %copy.140 = bf16[8,12,18,18]{3,2,0,1:T(8,128)(2,1)S(1)} copy(bf16[8,12,18,18]{1,3,2,0:T(8,128)(2,1)S(1)} %pad_maximum_fusion) | data formatting | bytes 124416 | tf_op jit(solution)/shard_map/concatenate | solution.py:71
  23.4 0.3 reshape.201
  23.7 1.1 %stack.8 = bf16[16,8,12,326]{3,1,2,0:T(8,128)(2,1)} broadcast(bf16[8,12,326]{2,0,1:T(8,128)(2,1)S(1)} %pad.24), dimensions={1,2,3} | broadcast | bytes 1064064 | tf_op jit(solution)/shard_map/stack | solution.py:11
  24.8 7.6 %all-to-all-start = ((bf16[16,8,12,326]{3,1,2,0:T(8,128)(2,1)}), bf16[16,8,12,326]{3,1,2,0:T(8,128)(2,1)S(1)}, u32[]{:S(2)}, u32[]{:S(2)}) async-start(bf16[16,8,12,326]{3,1,2,0:T(8,128)(2,1)} %stack.8), calls=%async_computation | async-start | bytes 2359296 | tf_op jit(solution)/shard_map/all_to_all | solution.py:12
  32.6 1.4 %scatter_custom_fusion = s32[192]{0:T(256)S(1)} fusion(s32[256]{0:T(256)S(1)} %compare_select_fusion.1, s32[256]{0:T(256)S(1)} %iota.13, s32[]{:T(128)} %constant.105.clone.1), kind=kCustom, calls=%fused_computation.181 | custom fusion | bytes 772 | tf_op jit(solution)/shard_map/scatter | solution.py:157
  34.1 0.6 gather_fusion.1
  34.7 0.6 gather_fusion.3
  35.5 0.6 dynamic_slice.19
  36.3 0.6 dynamic_slice.18
  38.7 8.9 %all-to-all-done = bf16[16,8,12,326]{3,1,2,0:T(8,128)(2,1)S(1)} async-done(((bf16[16,8,12,326]{3,1,2,0:T(8,128)(2,1)}), bf16[16,8,12,326]{3,1,2,0:T(8,128)(2,1)S(1)}, u32[]{:S(2)}, u32[]{:S(2)}) %all-to-all-start) | async-done | bytes 1001504 | tf_op jit(solution)/shard_map/all_to_all | solution.py:12
  47.5 3.0 %fusion.131 = (bf16[8,192,288]{2,0,1:T(8,128)(2,1)S(1)}, bf16[8,192,288]{2,0,1:T(8,128)(2,1)S(1)}, bf16[8,192,288]{2,0,1:T(8,128)(2,1)S(1)}, bf16[8,192,288]{2,0...) fusion(bf16[8,192,326]{2,0,1:T(8,128)(2,1)S(1)} %bitcast.185), kind=kLoop, calls=%fused_computation.184 | loop fusion | bytes 15925248 | tf_op jit(solution)/shard_map/slice | solution.py:92
  51.0 0.3 fusion.6
  51.3 0.3 fusion.8
  51.6 0.3 fusion.10
  51.9 0.3 fusion.12
  52.7 0.3 fusion.42
  53.0 0.5 reshape.204
  53.5 0.3 reshape.205
  54.0 0.6 gather_fusion.4
  54.6 2.1 %collective-permute-start.2 = (bf16[6,5632]{1,0:T(8,128)(2,1)S(1)}, bf16[6,5632]{1,0:T(8,128)(2,1)S(1)}, u32[]{:S(2)}, u32[]{:S(2)}) collective-permute-start(bf16[6,5632]{1,0:T(8,128)(2,1)S(1)} %gather_fusion.4), channel_id=1, source_target_pairs={{0,16},{16,0},{32,48},{48,32},{64,80},{80,64},{96,112},{112,96},{1... | collective-permute-start | bytes 202760 | tf_op jit(solution)/shard_map/ppermute | solution.py:35
  56.7 0.7 compare_and_fusion
  57.3 0.6 gather_fusion.2
  58.7 0.4 copy.158
  59.1 0.4 copy.157
  59.5 0.4 pad_maximum_fusion.2
  60.1 22.5 %all_gather.6 = bf16[6,128,326]{2,1,0:T(8,128)(2,1)S(1)} all-gather(bf16[6,8,326]{2,1,0:T(8,128)(2,1)S(1)} %pad.27), channel_id=1, replica_groups=mesh['tiles'=32,'chan'=16] {'chan'}, dimensions={1}, use_global_device_ids=true | all-gather | bytes 532032 | tf_op jit(solution)/shard_map/all_gather | solution.py:103
  82.8 0.4 convolution_add_fusion.7
  83.1 0.4 convolution_add_fusion.6
  83.5 0.4 convolution_add_fusion.5
  83.9 0.4 convolution_add_fusion.4
  84.2 0.4 convolution_add_fusion.3
  84.6 0.4 convolution_add_fusion.2
  84.9 0.4 convolution_add_fusion.1
  85.3 0.4 fusion.45
  86.1 22.6 %all_gather.7 = bf16[6,192,256]{2,0,1:T(8,128)(2,1)S(1)} all-gather(bf16[6,12,256]{2,0,1:T(8,128)(2,1)S(1)} %copy.171), channel_id=1, replica_groups=mesh['tiles'=32,'chan'=16] {'chan'}, dimensions={1}, use_global_device_ids=true | all-gather | bytes 626688 | tf_op jit(solution)/shard_map/all_gather | solution.py:108
  108.7 0.8 add_convert_fusion
  (102 shorter events, 6.8 us)
Async XLA Ops:
  0.6 108.0 %copy-start = (bf16[8,192]{1,0:T(8,128)(2,1)S(1)}, bf16[8,192]{1,0:T(8,128)(2,1)}, u32[]{:S(2)}) copy-start(bf16[8,192]{1,0:T(8,128)(2,1)} %param.12) | copy-start | bytes 9220
  2.7 11.8 %copy-start.5 = (s32[256]{0:T(256)S(1)}, s32[256]{0:T(256)}, u32[]{:S(2)}) copy-start(s32[256]{0:T(256)} %param.13) | copy-start | bytes 3076
  2.7 12.2 %copy-start.6 = (s32[256,4]{0,1:T(4,128)S(1)}, s32[256,4]{0,1:T(4,128)}, u32[]{:S(2)}) copy-start(s32[256,4]{0,1:T(4,128)} %param.14) | copy-start | bytes 12292
  2.7 12.5 %copy-start.7 = (s32[256,4]{0,1:T(4,128)S(1)}, s32[256,4]{0,1:T(4,128)}, u32[]{:S(2)}) copy-start(s32[256,4]{0,1:T(4,128)} %param.15) | copy-start | bytes 12292
  5.5 13.8 %collective-permute-start.1 = (bf16[8,1280]{1,0:T(8,128)(2,1)S(1)}, bf16[8,1280]{1,0:T(8,128)(2,1)S(1)}, u32[]{:S(2)}, u32[]{:S(2)}) collective-permute-start(bf16[8,1280]{1,0:T(8,128)(2,1)S(1)} %reshape.200), channel_id=1, source_target_pairs={{16,0},{32,16},{48,32},{64,48},{80,64},{96,80},{112,96},{128,112},... | collective-permute-start | bytes 61448 | tf_op jit(solution)/shard_map/ppermute | solution.py:25
  14.5 4.4 %collective-permute-start = (bf16[8,1280]{1,0:T(8,128)(2,1)S(1)}, bf16[8,1280]{1,0:T(8,128)(2,1)S(1)}, u32[]{:S(2)}, u32[]{:S(2)}) collective-permute-start(bf16[8,1280]{1,0:T(8,128)(2,1)S(1)} %reshape.200), channel_id=1, source_target_pairs={{0,16},{16,32},{32,48},{48,64},{64,80},{80,96},{96,112},{112,128},... | collective-permute-start | bytes 61448 | tf_op jit(solution)/shard_map/ppermute | solution.py:23
  24.8 7.8 %copy-start.3 = (bf16[8,8,256]{2,1,0:T(8,128)(2,1)S(1)}, bf16[8,8,256]{2,1,0:T(8,128)(2,1)}, u32[]{:S(2)}) copy-start(bf16[8,8,256]{2,1,0:T(8,128)(2,1)} %param.9) | copy-start | bytes 98308
  24.8 22.7 %all-to-all-start = ((bf16[16,8,12,326]{3,1,2,0:T(8,128)(2,1)}), bf16[16,8,12,326]{3,1,2,0:T(8,128)(2,1)S(1)}, u32[]{:S(2)}, u32[]{:S(2)}) async-start(bf16[16,8,12,326]{3,1,2,0:T(8,128)(2,1)} %stack.8), calls=%async_computation | async-start | bytes 2359296 | tf_op jit(solution)/shard_map/all_to_all | solution.py:12
  47.5 3.0 %copy-start.8 = (bf16[9,12,192]{2,1,0:T(8,128)(2,1)S(1)}, bf16[9,12,192]{2,1,0:T(8,128)(2,1)}, u32[]{:S(2)}) copy-start(bf16[9,12,192]{2,1,0:T(8,128)(2,1)} %param.10) | copy-start | bytes 124420
  53.0 0.9 copy-start.1
  53.9 4.1 %copy-start.2 = (bf16[8,12,256]{2,0,1:T(8,128)(2,1)}, bf16[8,12,256]{2,0,1:T(8,128)(2,1)S(1)}, u32[]{:S(2)}) copy-start(bf16[8,12,256]{2,0,1:T(8,128)(2,1)S(1)} %fusion.69) | copy-start | bytes 147460
  54.6 3.4 %collective-permute-start.2 = (bf16[6,5632]{1,0:T(8,128)(2,1)S(1)}, bf16[6,5632]{1,0:T(8,128)(2,1)S(1)}, u32[]{:S(2)}, u32[]{:S(2)}) collective-permute-start(bf16[6,5632]{1,0:T(8,128)(2,1)S(1)} %gather_fusion.4), channel_id=1, source_target_pairs={{0,16},{16,0},{32,48},{48,32},{64,80},{80,64},{96,112},{112,96},{1... | collective-permute-start | bytes 202760 | tf_op jit(solution)/shard_map/ppermute | solution.py:35
  58.7 23.9 %copy-start.4 = (bf16[9,8,128]{2,1,0:T(8,128)(2,1)S(1)}, bf16[9,8,128]{2,1,0:T(8,128)(2,1)}, u32[]{:S(2)}) copy-start(bf16[9,8,128]{2,1,0:T(8,128)(2,1)} %param.11) | copy-start | bytes 55300
